TPU v7x, 1024 devices: a whole 4x4x32 slice. The times are simulated.
1024 devices in a mesh: ctx: 128 (over z, y), ch: 8 (over x, core).
Axes of the slice: x: 4, y: 4, z: 32, core: 2. Of those that a mesh axis runs over, the one named last changes fastest.
Arguments:
- features: bfloat16 [3, 16384, 8192], P(None, 'ctx', 'ch'), may hold values from -6 to 6
- grad_rows: bfloat16 [16384, 8192], P(('ctx', 'ch')), may hold values from -6 to 6
- conv_taps: float32 [3, 3, 8192], P(None, None, 'ch'), may hold values from -3.5 to 3.5
- decay_rate: float32 [16, 8192], P(None, 'ch'), may hold values from 0 to 1, as said below
- residue: float32 [16, 8192], P(None, 'ch'), may hold values from -1.5 to 1.5
- skip_gain: float32 [8192], P('ch'), may hold values from -1 to 1
Outputs:
- grad_features: bfloat16 [3, 16384, 8192], P(None, 'ctx', 'ch')
Inputs may be any that keep to these rules, and one draw needn't show every extreme that they name: `decay_rate`: positive decay rates.
All inputs are finite; a program needn't handle non-finite values.
Results may differ from a plain program's by a relative error of at most 0.00125.
Values may be sent and summed in bfloat16 or wider, within the bound.
No kernel may reach another device: no remote copies, remote signals or barrier semaphores. Data moves between devices by JAX's collectives and lax.ppermute only.
A program may use at most 128 MiB of HBM per device.

v0:
```python
import math

import jax
import jax.numpy as jnp
from jax import lax
from jax.sharding import PartitionSpec as P


def shifted(block, axis, distance):
    devices = range(lax.axis_size(axis))
    route = [(i - distance, i) for i in devices if i - distance in devices]
    return lax.ppermute(block, axis, route)


def carried_in(value, axis, join, neutral, backward):
    count, mine = (lax.axis_size(axis), lax.axis_index(axis))
    pieces = jax.tree.map(lambda part: lax.all_gather(part, axis), value)
    if backward:
        pieces = jax.tree.map(lambda part: part[::-1], pieces)
        mine = count - 1 - mine
    total = jax.tree.map(
        lambda part, zero: jnp.full_like(part, 0) + jnp.asarray(zero, part.dtype), value, neutral
    )

    def turn(position, total):
        longer = join(total, jax.tree.map(lambda part: part[position], pieces))
        return jax.tree.map(lambda new, old: jnp.where(position < mine, new, old), longer, total)

    return lax.fori_loop(0, count - 1, turn, total)


def local_pass(signal, decay_rate, gain_in, gain_out):
    total_len, width_dev = signal.shape
    block_len = math.gcd(16, total_len)
    block_count = total_len // block_len
    offsets = jnp.arange(block_len, dtype=jnp.float32)
    rates = decay_rate[None]
    decay_in = jnp.exp(-rates * (block_len - 1.0 - offsets)[:, None, None]) * gain_in[None]
    decay_out = jnp.exp(-rates * (offsets + 1.0)[:, None, None]) * gain_out[None]
    kernel = jnp.sum(jnp.exp(-rates * offsets[:, None, None]) * (gain_in * gain_out)[None], axis=1)
    lag_index = (
        jnp.arange(block_len, dtype=jnp.int32)[:, None]
        - jnp.arange(block_len, dtype=jnp.int32)[None, :]
    )
    toeplitz = jnp.where(
        lag_index[:, :, None] >= 0,
        kernel[jnp.maximum(lag_index, 0)],
        jnp.zeros_like(kernel[:1, None]),
    )
    blocks = signal.reshape(block_count, block_len, width_dev)
    local_out = jnp.sum(blocks[:, None, :, :] * toeplitz[None], axis=2)
    block_ends = jnp.sum(blocks[:, :, None, :] * decay_in[None], axis=1)
    block_decay = jnp.exp(-decay_rate * block_len)

    def advance(state_now, entry):
        return (block_decay * state_now + entry, state_now)

    final_state, block_starts = lax.scan(advance, jnp.zeros_like(decay_rate), block_ends)
    return (local_out, block_starts, final_state, decay_out)


def finish(pieces, decay_rate, initial):
    local_out, block_starts, final_state, decay_out = pieces
    block_count, block_len, width_dev = local_out.shape
    anchors = jnp.arange(block_count, dtype=jnp.float32) * block_len
    powers = jnp.exp(-decay_rate[None] * anchors[:, None, None])
    states = block_starts + powers * initial[None]
    result = local_out + jnp.sum(decay_out[None] * states[:, None], axis=2)
    return result.reshape(block_count * block_len, width_dev)


def per_device(features, grad_rows, conv_taps, decay_rate, residue, skip_gain):
    length = features.shape[1]
    rim_rows = conv_taps.shape[1] - 1
    grad_out = lax.all_to_all(grad_rows, "ch", split_axis=1, concat_axis=0, tiled=True)
    last_rows = features[:, length - rim_rows :, :]
    before = shifted(last_rows, "ctx", 1)
    extended = jnp.concatenate([before, features], axis=1)
    featurized = conv_taps[:, 0, None, :] * extended[:, rim_rows : rim_rows + length, :]
    for shift_by in range(1, rim_rows + 1):
        featurized = (
            featurized
            + conv_taps[:, shift_by, None, :]
            * extended[:, rim_rows - shift_by : rim_rows - shift_by + length, :]
        )
    queries = featurized[0]
    keys_feat = featurized[1]
    values_feat = featurized[2]
    gain_in = jnp.sqrt(-jnp.expm1(-2.0 * decay_rate))
    product = keys_feat * values_feat
    forward = local_pass(product, decay_rate, gain_in, residue)
    grad_float = grad_out.astype(jnp.float32)
    grad_conv = grad_float * queries
    backward = local_pass(grad_conv[::-1], decay_rate, jnp.ones_like(decay_rate), residue * gain_in)

    def combine(earlier, later):
        return (
            earlier[0] + later[0],
            jnp.exp(-decay_rate * (length * later[0])) * earlier[1] + later[1],
        )

    single = jnp.ones((), jnp.float32)
    identity = (jnp.zeros((), jnp.float32), jnp.zeros_like(decay_rate))
    state_in = carried_in((single, forward[2]), "ctx", combine, identity, False)[1]
    adjoint_in = carried_in((single, backward[2]), "ctx", combine, identity, True)[1]
    conv_out = finish(forward, decay_rate, state_in) + skip_gain[None] * product
    grad_query = grad_float * conv_out
    grad_product = finish(backward, decay_rate, adjoint_in)[::-1] + skip_gain[None] * grad_conv
    grad_key = grad_product * values_feat
    grad_value = grad_product * keys_feat
    grad_stack = jnp.stack([grad_query, grad_key, grad_value])
    following = shifted(grad_stack[:, :rim_rows, :], "ctx", -1)
    padded = jnp.concatenate([grad_stack, following], axis=1)
    result = conv_taps[:, 0, None, :] * padded[:, 0:length, :]
    for shift_by in range(1, rim_rows + 1):
        result = (
            result + conv_taps[:, shift_by, None, :] * padded[:, shift_by : shift_by + length, :]
        )
    return result.astype(jnp.bfloat16)


def solution(mesh):
    in_specs = (
        P(None, "ctx", "ch"),
        P(("ctx", "ch"), None),
        P(None, None, "ch"),
        P(None, "ch"),
        P(None, "ch"),
        P("ch"),
    )
    out_specs = P(None, "ctx", "ch")
    return jax.shard_map(
        per_device, mesh=mesh, in_specs=in_specs, out_specs=out_specs, check_vma=False
    )
```

profile of v0, /device:TPU:28, one launch (start us, length us, event | category | flops | bytes accessed | tf_op | source)
XLA Modules:
  0.0 923.8 jit_solution(1438512062060250488)
XLA Ops:
  7.4 3.5 collective-permute-start
  10.9 1.7 copy.18
  12.6 4.8 all-to-all-start
  17.4 0.9 fusion.12
  19.4 2.3 fusion.5
  21.7 1.1 gather_fusion
  22.8 1.1 broadcast_select_fusion
  24.0 2.5 multiply_add_fusion
  27.5 7.8 multiply_reduce_fusion.5
  35.4 7.3 while.60
  43.4 1.4 dynamic-slice
  45.6 286.3 %all-reduce = f32[128]{0:T(128)S(1)} all-reduce(f32[128]{0:T(128)S(1)} %dynamic-update-slice), channel_id=1, replica_groups=mesh['ctx'=128,'ch'=8] {'ctx'}, use_global_device_ids=true, to_apply=%add | all-reduce | flops 128 | bytes 1024
  332.0 7.3 while.58
  340.0 8.3 rev.14
  348.3 261.9 %while.61 = (s32[]{:T(128)}, f32[16,1024]{1,0:T(8,128)S(1)}, s32[]{:T(128)}, f32[128]{0:T(128)S(1)}, f32[16,1024]{1,0:T(8,128)S(1)}, /*index=5*/f32[128,16,1024]{2,1,0:T(8,128)}, s32[]{:T(128)}, f32[1]{0:T(128)}, s32[]{:T(128)}) while((s32[]{:T(128)}, f32[16,1024]{1,0:T(8,128)S(1)}, s32[]{:T(128)}, f32[128]{0:T(128)S(1)}, ...), condition=%wide.region_13.14_spmd.clone, body=%wide.region_12.13_spmd.clone.sunk | while | flops 81925 | bytes 262289 | solution.py:29
  610.2 10.3 %all-gather.5.cloned.1.call-done = f32[2048,1024]{1,0:T(8,128)} async-done(((f32[16,1024]{1,0:T(8,128)}), f32[2048,1024]{1,0:T(8,128)}) %all-gather.5.cloned.1.call-update) | async-done | bytes 8388624 | tf_op jit(solution)/shard_map/all_gather | solution.py:17
  620.5 272.6 %while.59 = (s32[]{:T(128)}, f32[16,1024]{1,0:T(8,128)S(1)}, s32[]{:T(128)}, f32[128]{0:T(128)S(1)}, f32[16,1024]{1,0:T(8,128)S(1)}, /*index=5*/f32[128,16,1024]{2,1,0:T(8,128)}, s32[]{:T(128)}, f32[1]{0:T(128)}, s32[]{:T(128)}) while((s32[]{:T(128)}, f32[16,1024]{1,0:T(8,128)S(1)}, s32[]{:T(128)}, f32[128]{0:T(128)S(1)}, ...), condition=%wide.region_6.7_spmd.clone, body=%wide.region_5.6_spmd.clone.sunk | while | flops 81925 | bytes 262289 | solution.py:29
  893.1 2.3 multiply_add_fusion.3
  895.3 2.0 multiply_reduce_fusion
  898.3 4.8 rev.15
  903.0 3.1 multiply_reduce_fusion.3
  907.6 2.9 collective-permute-start.1
  910.5 4.9 collective-permute-done.1
  915.6 1.4 fusion.3
  (602 shorter events, 396.1 us)
Async XLA Ops:
  6.5 12.8 %copy-start.11 = (f32[16,1024]{1,0:T(8,128)S(1)}, f32[16,1024]{1,0:T(8,128)}, u32[]{:S(2)}) copy-start(f32[16,1024]{1,0:T(8,128)} %param.18) | copy-start | bytes 196612
  7.4 16.6 %collective-permute-start = (bf16[3,2,1024]{2,1,0:T(2,128)(2,1)S(1)}, bf16[3,2,1024]{2,1,0:T(2,128)(2,1)S(1)}, u32[]{:S(2)}, u32[]{:S(2)}) collective-permute-start(bf16[3,2,1024]{2,1,0:T(2,128)(2,1)S(1)} %slice.41), channel_id=1, source_target_pairs={{0,8},{8,16},{16,24},{24,32},{32,40},{40,48},{48,56},{56,64},{64,7... | collective-permute-start | bytes 36872 | tf_op jit(solution)/shard_map/ppermute | solution.py:12
  12.6 13.9 %all-to-all-start = ((bf16[16,8,1024]{2,0,1:T(8,128)(2,1)}), bf16[16,8,1024]{2,0,1:T(8,128)(2,1)S(1)}, u32[]{:S(2)}, u32[]{:S(2)}) async-start(bf16[16,8,1024]{2,0,1:T(8,128)(2,1)} %bitcast.63), calls=%async_computation | async-start | bytes 524288 | tf_op jit(solution)/shard_map/all_to_all | solution.py:75
  17.4 322.6 %all-gather.7.cloned.1.call-start = ((), (), s32[]{:S(2)}) async-start(), calls=%async_computation.2 | async-start | bytes 8454144 | tf_op jit(solution)/shard_map/all_gather | solution.py:17
  26.5 0.7 copy-start.4
  42.7 0.6 copy-start.1
  42.7 289.2 %copy-start.9 = (f32[8,16,1024]{2,1,0:T(8,128)}, f32[8,16,1024]{2,1,0:T(8,128)S(1)}, u32[]{:S(2)}) copy-start(f32[8,16,1024]{2,1,0:T(8,128)S(1)} %get-tuple-element.362) | copy-start | bytes 1572868
  43.3 577.2 %all-gather.5.cloned.1.call-start = ((), (), s32[]{:S(2)}) async-start(), calls=%async_computation.1 | async-start | bytes 8454144 | tf_op jit(solution)/shard_map/all_gather | solution.py:17
  339.3 0.6 copy-start
  339.3 8.9 copy-start.8
  620.5 274.8 %copy-start.3 = (f32[16,16,1024]{2,1,0:T(8,128)S(1)}, f32[16,16,1024]{2,1,0:T(8,128)}, u32[]{:S(2)}) copy-start(f32[16,16,1024]{2,1,0:T(8,128)} %get-tuple-element.493) | copy-start | bytes 3145732
  895.3 2.0 copy-start.7
  897.4 5.7 copy-start.2
  903.0 3.2 copy-start.6
  903.0 3.2 copy-start.10
  903.0 3.2 copy-start.12
  906.3 1.0 copy-start.5
  907.6 7.8 collective-permute-start.1
Sparse Core Ops, SparseCore 0:
  43.4 289.2 all-gather.6
  340.1 280.3 all-gather.4
where the time goes:
time: 940 us; the launch traced here: 924 us
  blocking collectives  286 us (30%)
  other arithmetic  262 us (28%)
  local copies, waits for them, and re-layouts  175 us (19%)
  loops' own time  161 us (17%)
  waiting for transfers between devices  15.3 us (2%)
  between operations  13.8 us (1%)
  starting transfers between devices  11.2 us (1%)
    unnamed x1, blocking collectives  286 us
    select_n x254, other arithmetic, turn(): jnp.where(position < mine, new, old)  222 us
    another operation x2, loops' own time, carried_in(): return lax.fori_loop(0, count - 1, turn, total)  160 us
    dynamic_slice x254, local copies, waits for them, and re-layouts, turn(): longer = join(total, jax.tree.map(lambda part: part[position], pieces))  152 us
  transfers between devices with their start and end apart: 5, of which 2 were waited for; matrix products, arithmetic and copies ran while one was open for 23% of the time, Pallas kernels for 0%

commit v1 on v0

--- a/solution.py
+++ b/solution.py
@@ -12,21 +12,19 @@
     return lax.ppermute(block, axis, route)
 
 
-def carried_in(value, axis, join, neutral, backward):
-    count, mine = (lax.axis_size(axis), lax.axis_index(axis))
-    pieces = jax.tree.map(lambda part: lax.all_gather(part, axis), value)
-    if backward:
-        pieces = jax.tree.map(lambda part: part[::-1], pieces)
-        mine = count - 1 - mine
-    total = jax.tree.map(
-        lambda part, zero: jnp.full_like(part, 0) + jnp.asarray(zero, part.dtype), value, neutral
-    )
-
-    def turn(position, total):
-        longer = join(total, jax.tree.map(lambda part: part[position], pieces))
-        return jax.tree.map(lambda new, old: jnp.where(position < mine, new, old), longer, total)
-
-    return lax.fori_loop(0, count - 1, turn, total)
+def carried_in(final, decay_rate, length, backward):
+    count = lax.axis_size("ctx")
+    step = -1 if backward else 1
+    factor = jnp.exp(-decay_rate * length)
+    total = shifted(final, "ctx", step)
+    if count > 2:
+        total = total + factor * shifted(final, "ctx", 2 * step)
+    distance = 2
+    while distance < count:
+        power = jnp.exp(-decay_rate * (length * distance))
+        total = total + power * shifted(total, "ctx", distance * step)
+        distance *= 2
+    return total
 
 
 def local_pass(signal, decay_rate, gain_in, gain_out):
@@ -93,16 +91,8 @@
     grad_conv = grad_float * queries
     backward = local_pass(grad_conv[::-1], decay_rate, jnp.ones_like(decay_rate), residue * gain_in)
 
-    def combine(earlier, later):
-        return (
-            earlier[0] + later[0],
-            jnp.exp(-decay_rate * (length * later[0])) * earlier[1] + later[1],
-        )
-
-    single = jnp.ones((), jnp.float32)
-    identity = (jnp.zeros((), jnp.float32), jnp.zeros_like(decay_rate))
-    state_in = carried_in((single, forward[2]), "ctx", combine, identity, False)[1]
-    adjoint_in = carried_in((single, backward[2]), "ctx", combine, identity, True)[1]
+    state_in = carried_in(forward[2], decay_rate, length, False)
+    adjoint_in = carried_in(backward[2], decay_rate, length, True)
     conv_out = finish(forward, decay_rate, state_in) + skip_gain[None] * product
     grad_query = grad_float * conv_out
     grad_product = finish(backward, decay_rate, adjoint_in)[::-1] + skip_gain[None] * grad_conv

time: 940 us -> 244 us (0.26)
  the two profiles are of different devices: /device:TPU:28 before, /device:TPU:112 now
where the time goes in v1:
time: 244 us; the launch traced here: 242 us
  starting transfers between devices  99 us (41%)
  waiting for transfers between devices  91.1 us (37%)
  other arithmetic  39.3 us (16%)
  local copies, waits for them, and re-layouts  11.2 us (5%)
    ppermute x18, starting transfers between devices, shifted(): return lax.ppermute(block, axis, route)  94.7 us
    ppermute x18, waiting for transfers between devices, shifted(): return lax.ppermute(block, axis, route)  91.1 us
    add x16, other arithmetic, advance(): return (block_decay * state_now + entry, state_now)  14.1 us
    reduce_sum x1, other arithmetic, local_pass(): local_out = jnp.sum(blocks[:, None, :, :] * toeplitz[None], axis=2)  7.77 us
    reduce_sum x2, other arithmetic, finish(): result = local_out + jnp.sum(decay_out[None] * states[:, None], axis=2)  5.16 us
  transfers between devices with their start and end apart: 19, of which 13 were waited for; matrix products, arithmetic and copies ran while one was open for 8% of the time, Pallas kernels for 0%

profile of v1, /device:TPU:112, one launch (start us, length us, event | category | flops | bytes accessed | tf_op | source)
XLA Modules:
  0.0 241.5 jit_solution(5120233333593663941)
XLA Ops:
  5.7 4.3 %all-to-all-start = ((bf16[16,8,1024]{2,0,1:T(8,128)(2,1)}), bf16[16,8,1024]{2,0,1:T(8,128)(2,1)S(1)}, u32[]{:S(2)}, u32[]{:S(2)}) async-start(bf16[16,8,1024]{2,0,1:T(8,128)(2,1)} %bitcast.50), calls=%async_computation | async-start | bytes 524288 | tf_op jit(solution)/shard_map/all_to_all | solution.py:73
  20.2 7.8 %multiply_reduce_fusion.5 = (f32[8,16,1024]{2,1,0:T(8,128)}, f32[8,16,1024]{2,1,0:T(8,128)}, f32[8,16,1024]{2,1,0:T(8,128)}, f32[8,16,1024]{2,1,0:T(8,128)}) fusion(f32[16,16,1024]{2,1,0:T(8,128)} %broadcast_select_fusion, f32[8,16,1024]{2,1,0:T(8,128)S(1)} %bitcast.61, f32[8,16,1024]{2,1,0:T(8,128)S(1)} %bitcast.62, f32[16,16,1024]{2,1,0:T(8,128)} %get-tuple-element.136, ...), kind=kLoop, calls=%fused_computation.10 | loop fusion | flops 16252928 | bytes 6291456 | tf_op jit(solution)/shard_map/reduce_sum | solution.py:49
  28.0 7.3 %while.26 = (s32[]{:T(128)}, f32[16,1024]{1,0:T(8,128)S(1)}, f32[8,16,1024]{2,1,0:T(8,128)S(1)}, f32[16,1024]{1,0:T(8,128)S(1)}, f32[8,16,1024]{2,1,0:T(8,128)}, /*index=5*/s32[]{:T(128)}, s32[]{:T(128)}) while((s32[]{:T(128)}, f32[16,1024]{1,0:T(8,128)S(1)}, f32[8,16,1024]{2,1,0:T(8,128)S(1)}, f32[16,1024]{1,0:T(8,128)S(1)}, ...), condition=%wide.region_4.5_spmd.clone, body=%wide.region_3.4_spmd.clone.sunk | while | flops 65539 | bytes 393312 | solution.py:56
  35.3 4.7 %collective-permute-start.1 = (f32[16,1024]{1,0:T(8,128)S(1)}, f32[16,1024]{1,0:T(8,128)S(1)}, u32[]{:S(2)}, u32[]{:S(2)}) collective-permute-start(f32[16,1024]{1,0:T(8,128)S(1)} %get-tuple-element.62), channel_id=1, source_target_pairs={{0,8},{8,16},{16,24},{24,32},{32,40},{40,48},{48,56},{56,64},{64,7... | collective-permute-start | bytes 196616 | tf_op jit(solution)/shard_map/ppermute | solution.py:12
  40.0 3.9 %collective-permute-start.2 = (f32[16,1024]{1,0:T(8,128)S(1)}, f32[16,1024]{1,0:T(8,128)S(1)}, u32[]{:S(2)}, u32[]{:S(2)}) collective-permute-start(f32[16,1024]{1,0:T(8,128)S(1)} %get-tuple-element.62), channel_id=1, source_target_pairs={{0,16},{8,24},{16,32},{24,40},{32,48},{40,56},{48,64},{56,72},{64,... | collective-permute-start | bytes 196616 | tf_op jit(solution)/shard_map/ppermute | solution.py:12
  43.9 3.8 %collective-permute-done.2 = f32[16,1024]{1,0:T(8,128)S(1)} collective-permute-done((f32[16,1024]{1,0:T(8,128)S(1)}, f32[16,1024]{1,0:T(8,128)S(1)}, u32[]{:S(2)}, u32[]{:S(2)}) %collective-permute-start.2) | collective-permute-done | bytes 65568 | tf_op jit(solution)/shard_map/ppermute | solution.py:12
  47.7 6.0 %collective-permute-start.3 = (f32[16,1024]{1,0:T(8,128)S(1)}, f32[16,1024]{1,0:T(8,128)S(1)}, u32[]{:S(2)}, u32[]{:S(2)}) collective-permute-start(f32[16,1024]{1,0:T(8,128)S(1)} %multiply_add_fusion.17), channel_id=1, source_target_pairs={{0,16},{8,24},{16,32},{24,40},{32,48},{40,56},{48,64},{56,72},{64,... | collective-permute-start | bytes 196616 | tf_op jit(solution)/shard_map/ppermute | solution.py:12
  55.6 3.6 %collective-permute-start.4 = (f32[16,1024]{1,0:T(8,128)S(1)}, f32[16,1024]{1,0:T(8,128)S(1)}, u32[]{:S(2)}, u32[]{:S(2)}) collective-permute-start(f32[16,1024]{1,0:T(8,128)S(1)} %multiply_add_fusion.16), channel_id=1, source_target_pairs={{0,32},{8,40},{16,48},{24,56},{32,64},{40,72},{48,80},{56,88},{64,... | collective-permute-start | bytes 196616 | tf_op jit(solution)/shard_map/ppermute | solution.py:12
  61.8 5.0 %collective-permute-start.5 = (f32[16,1024]{1,0:T(8,128)S(1)}, f32[16,1024]{1,0:T(8,128)S(1)}, u32[]{:S(2)}, u32[]{:S(2)}) collective-permute-start(f32[16,1024]{1,0:T(8,128)S(1)} %multiply_add_fusion.15), channel_id=1, source_target_pairs={{0,64},{8,72},{16,80},{24,88},{32,96},{40,104},{48,112},{56,120},{... | collective-permute-start | bytes 196616 | tf_op jit(solution)/shard_map/ppermute | solution.py:12
  68.9 9.4 %collective-permute-start.6 = (f32[16,1024]{1,0:T(8,128)S(1)}, f32[16,1024]{1,0:T(8,128)S(1)}, u32[]{:S(2)}, u32[]{:S(2)}) collective-permute-start(f32[16,1024]{1,0:T(8,128)S(1)} %multiply_add_fusion.14), channel_id=1, source_target_pairs={{0,128},{8,136},{16,144},{24,152},{32,160},{40,168},{48,176},{56,1... | collective-permute-start | bytes 196616 | tf_op jit(solution)/shard_map/ppermute | solution.py:12
  81.2 16.5 %collective-permute-start.7 = (f32[16,1024]{1,0:T(8,128)S(1)}, f32[16,1024]{1,0:T(8,128)}, u32[]{:S(2)}, u32[]{:S(2)}) collective-permute-start(f32[16,1024]{1,0:T(8,128)S(1)} %multiply_add_fusion.13), channel_id=1, source_target_pairs={{0,256},{8,264},{16,272},{24,280},{32,288},{40,296},{48,304},{56,3... | collective-permute-start | bytes 196616 | tf_op jit(solution)/shard_map/ppermute | solution.py:12
  97.7 7.3 %while.27 = (s32[]{:T(128)}, f32[16,1024]{1,0:T(8,128)S(1)}, f32[8,16,1024]{2,1,0:T(8,128)S(1)}, f32[16,1024]{1,0:T(8,128)S(1)}, f32[8,16,1024]{2,1,0:T(8,128)}, /*index=5*/s32[]{:T(128)}, s32[]{:T(128)}) while((s32[]{:T(128)}, f32[16,1024]{1,0:T(8,128)S(1)}, f32[8,16,1024]{2,1,0:T(8,128)S(1)}, f32[16,1024]{1,0:T(8,128)S(1)}, ...), condition=%wide.region_9.10_spmd.clone, body=%wide.region_8.9_spmd.clone.sunk | while | flops 65539 | bytes 393312 | solution.py:56
  105.1 5.6 %collective-permute-start.10 = (f32[16,1024]{1,0:T(8,128)S(1)}, f32[16,1024]{1,0:T(8,128)S(1)}, u32[]{:S(2)}, u32[]{:S(2)}) collective-permute-start(f32[16,1024]{1,0:T(8,128)S(1)} %get-tuple-element.64), channel_id=1, source_target_pairs={{16,0},{24,8},{32,16},{40,24},{48,32},{56,40},{64,48},{72,56},{80,... | collective-permute-start | bytes 196616 | tf_op jit(solution)/shard_map/ppermute | solution.py:12
  113.5 13.3 %collective-permute-start.8 = (f32[16,1024]{1,0:T(8,128)S(1)}, f32[16,1024]{1,0:T(8,128)S(1)}, u32[]{:S(2)}, u32[]{:S(2)}) collective-permute-start(f32[16,1024]{1,0:T(8,128)S(1)} %multiply_add_fusion.12), channel_id=1, source_target_pairs={{0,512},{8,520},{16,528},{24,536},{32,544},{40,552},{48,560},{56,5... | collective-permute-start | bytes 196616 | tf_op jit(solution)/shard_map/ppermute | solution.py:12
  128.8 6.2 %collective-permute-start.11 = (f32[16,1024]{1,0:T(8,128)S(1)}, f32[16,1024]{1,0:T(8,128)S(1)}, u32[]{:S(2)}, u32[]{:S(2)}) collective-permute-start(f32[16,1024]{1,0:T(8,128)S(1)} %get-tuple-element.135), channel_id=1, source_target_pairs={{16,0},{24,8},{32,16},{40,24},{48,32},{56,40},{64,48},{72,56},{80,... | collective-permute-start | bytes 196616 | tf_op jit(solution)/shard_map/ppermute | solution.py:12
  134.9 4.2 %collective-permute-done.11 = f32[16,1024]{1,0:T(8,128)S(1)} collective-permute-done((f32[16,1024]{1,0:T(8,128)S(1)}, f32[16,1024]{1,0:T(8,128)S(1)}, u32[]{:S(2)}, u32[]{:S(2)}) %collective-permute-start.11) | collective-permute-done | bytes 65568 | tf_op jit(solution)/shard_map/ppermute | solution.py:12
  141.4 5.1 %collective-permute-done.12 = f32[16,1024]{1,0:T(8,128)S(1)} collective-permute-done((f32[16,1024]{1,0:T(8,128)S(1)}, f32[16,1024]{1,0:T(8,128)S(1)}, u32[]{:S(2)}, u32[]{:S(2)}) %collective-permute-start.12) | collective-permute-done | bytes 65568 | tf_op jit(solution)/shard_map/ppermute | solution.py:12
  146.6 7.3 %collective-permute-start.13 = (f32[16,1024]{1,0:T(8,128)S(1)}, f32[16,1024]{1,0:T(8,128)S(1)}, u32[]{:S(2)}, u32[]{:S(2)}) collective-permute-start(f32[16,1024]{1,0:T(8,128)S(1)} %multiply_add_fusion.8), channel_id=1, source_target_pairs={{64,0},{72,8},{80,16},{88,24},{96,32},{104,40},{112,48},{120,56},{... | collective-permute-start | bytes 196616 | tf_op jit(solution)/shard_map/ppermute | solution.py:12
  153.9 3.4 %collective-permute-done.13 = f32[16,1024]{1,0:T(8,128)S(1)} collective-permute-done((f32[16,1024]{1,0:T(8,128)S(1)}, f32[16,1024]{1,0:T(8,128)S(1)}, u32[]{:S(2)}, u32[]{:S(2)}) %collective-permute-start.13) | collective-permute-done | bytes 65568 | tf_op jit(solution)/shard_map/ppermute | solution.py:12
  158.8 8.8 %collective-permute-done.14 = f32[16,1024]{1,0:T(8,128)S(1)} collective-permute-done((f32[16,1024]{1,0:T(8,128)S(1)}, f32[16,1024]{1,0:T(8,128)S(1)}, u32[]{:S(2)}, u32[]{:S(2)}) %collective-permute-start.14) | collective-permute-done | bytes 65568 | tf_op jit(solution)/shard_map/ppermute | solution.py:12
  168.9 26.7 %collective-permute-done.15 = f32[16,1024]{1,0:T(8,128)S(1)} collective-permute-done((f32[16,1024]{1,0:T(8,128)S(1)}, f32[16,1024]{1,0:T(8,128)S(1)}, u32[]{:S(2)}, u32[]{:S(2)}) %collective-permute-start.15) | collective-permute-done | bytes 65568 | tf_op jit(solution)/shard_map/ppermute | solution.py:12
  197.0 24.0 %collective-permute-done.16 = f32[16,1024]{1,0:T(8,128)S(1)} collective-permute-done((f32[16,1024]{1,0:T(8,128)S(1)}, f32[16,1024]{1,0:T(8,128)S(1)}, u32[]{:S(2)}, u32[]{:S(2)}) %collective-permute-start.16) | collective-permute-done | bytes 65568 | tf_op jit(solution)/shard_map/ppermute | solution.py:12
  225.0 4.8 %rev.7 = f32[128,1024]{1,0:T(8,128)} reverse(f32[128,1024]{1,0:T(8,128)} %bitcast.64), dimensions={0} | reverse | bytes 1048576 | tf_op jit(solution)/shard_map/rev | solution.py:98
  236.2 3.8 %collective-permute-done.17 = f32[3,2,1024]{2,1,0:T(2,128)S(1)} collective-permute-done((f32[3,2,1024]{2,1,0:T(2,128)S(1)}, f32[3,2,1024]{2,1,0:T(2,128)S(1)}, u32[]{:S(2)}, u32[]{:S(2)}) %collective-permute-start.17) | collective-permute-done | bytes 24608 | tf_op jit(solution)/shard_map/ppermute | solution.py:12
  (117 shorter events, 62.6 us)
Async XLA Ops:
  0.0 12.0 %copy-start.8 = (f32[16,1024]{1,0:T(8,128)S(1)}, f32[16,1024]{1,0:T(8,128)}, u32[]{:S(2)}) copy-start(f32[16,1024]{1,0:T(8,128)} %param.14) | copy-start | bytes 196612
  0.9 15.7 %collective-permute-start = (bf16[3,2,1024]{2,1,0:T(2,128)(2,1)S(1)}, bf16[3,2,1024]{2,1,0:T(2,128)(2,1)S(1)}, u32[]{:S(2)}, u32[]{:S(2)}) collective-permute-start(bf16[3,2,1024]{2,1,0:T(2,128)(2,1)S(1)} %slice.41), channel_id=1, source_target_pairs={{0,8},{8,16},{16,24},{24,32},{32,40},{40,48},{48,56},{56,64},{64,7... | collective-permute-start | bytes 36872 | tf_op jit(solution)/shard_map/ppermute | solution.py:12
  5.7 13.4 %all-to-all-start = ((bf16[16,8,1024]{2,0,1:T(8,128)(2,1)}), bf16[16,8,1024]{2,0,1:T(8,128)(2,1)S(1)}, u32[]{:S(2)}, u32[]{:S(2)}) async-start(bf16[16,8,1024]{2,0,1:T(8,128)(2,1)} %bitcast.50), calls=%async_computation | async-start | bytes 524288 | tf_op jit(solution)/shard_map/all_to_all | solution.py:73
  28.0 19.7 %copy-start = (f32[16,1024]{1,0:T(8,128)S(1)}, f32[16,1024]{1,0:T(8,128)}, u32[]{:S(2)}) copy-start(f32[16,1024]{1,0:T(8,128)} %param.13) | copy-start | bytes 196612
  35.3 8.6 %collective-permute-start.1 = (f32[16,1024]{1,0:T(8,128)S(1)}, f32[16,1024]{1,0:T(8,128)S(1)}, u32[]{:S(2)}, u32[]{:S(2)}) collective-permute-start(f32[16,1024]{1,0:T(8,128)S(1)} %get-tuple-element.62), channel_id=1, source_target_pairs={{0,8},{8,16},{16,24},{24,32},{32,40},{40,48},{48,56},{56,64},{64,7... | collective-permute-start | bytes 196616 | tf_op jit(solution)/shard_map/ppermute | solution.py:12
  40.0 7.7 %collective-permute-start.2 = (f32[16,1024]{1,0:T(8,128)S(1)}, f32[16,1024]{1,0:T(8,128)S(1)}, u32[]{:S(2)}, u32[]{:S(2)}) collective-permute-start(f32[16,1024]{1,0:T(8,128)S(1)} %get-tuple-element.62), channel_id=1, source_target_pairs={{0,16},{8,24},{16,32},{24,40},{32,48},{40,56},{48,64},{56,72},{64,... | collective-permute-start | bytes 196616 | tf_op jit(solution)/shard_map/ppermute | solution.py:12
  47.7 7.9 %collective-permute-start.3 = (f32[16,1024]{1,0:T(8,128)S(1)}, f32[16,1024]{1,0:T(8,128)S(1)}, u32[]{:S(2)}, u32[]{:S(2)}) collective-permute-start(f32[16,1024]{1,0:T(8,128)S(1)} %multiply_add_fusion.17), channel_id=1, source_target_pairs={{0,16},{8,24},{16,32},{24,40},{32,48},{40,56},{48,64},{56,72},{64,... | collective-permute-start | bytes 196616 | tf_op jit(solution)/shard_map/ppermute | solution.py:12
  55.6 6.2 %collective-permute-start.4 = (f32[16,1024]{1,0:T(8,128)S(1)}, f32[16,1024]{1,0:T(8,128)S(1)}, u32[]{:S(2)}, u32[]{:S(2)}) collective-permute-start(f32[16,1024]{1,0:T(8,128)S(1)} %multiply_add_fusion.16), channel_id=1, source_target_pairs={{0,32},{8,40},{16,48},{24,56},{32,64},{40,72},{48,80},{56,88},{64,... | collective-permute-start | bytes 196616 | tf_op jit(solution)/shard_map/ppermute | solution.py:12
  61.8 7.1 %collective-permute-start.5 = (f32[16,1024]{1,0:T(8,128)S(1)}, f32[16,1024]{1,0:T(8,128)S(1)}, u32[]{:S(2)}, u32[]{:S(2)}) collective-permute-start(f32[16,1024]{1,0:T(8,128)S(1)} %multiply_add_fusion.15), channel_id=1, source_target_pairs={{0,64},{8,72},{16,80},{24,88},{32,96},{40,104},{48,112},{56,120},{... | collective-permute-start | bytes 196616 | tf_op jit(solution)/shard_map/ppermute | solution.py:12
  68.9 12.3 %collective-permute-start.6 = (f32[16,1024]{1,0:T(8,128)S(1)}, f32[16,1024]{1,0:T(8,128)S(1)}, u32[]{:S(2)}, u32[]{:S(2)}) collective-permute-start(f32[16,1024]{1,0:T(8,128)S(1)} %multiply_add_fusion.14), channel_id=1, source_target_pairs={{0,128},{8,136},{16,144},{24,152},{32,160},{40,168},{48,176},{56,1... | collective-permute-start | bytes 196616 | tf_op jit(solution)/shard_map/ppermute | solution.py:12
  81.2 31.4 %collective-permute-start.7 = (f32[16,1024]{1,0:T(8,128)S(1)}, f32[16,1024]{1,0:T(8,128)}, u32[]{:S(2)}, u32[]{:S(2)}) collective-permute-start(f32[16,1024]{1,0:T(8,128)S(1)} %multiply_add_fusion.13), channel_id=1, source_target_pairs={{0,256},{8,264},{16,272},{24,280},{32,288},{40,296},{48,304},{56,3... | collective-permute-start | bytes 196616 | tf_op jit(solution)/shard_map/ppermute | solution.py:12
  105.1 21.8 %collective-permute-start.10 = (f32[16,1024]{1,0:T(8,128)S(1)}, f32[16,1024]{1,0:T(8,128)S(1)}, u32[]{:S(2)}, u32[]{:S(2)}) collective-permute-start(f32[16,1024]{1,0:T(8,128)S(1)} %get-tuple-element.64), channel_id=1, source_target_pairs={{16,0},{24,8},{32,16},{40,24},{48,32},{56,40},{64,48},{72,56},{80,... | collective-permute-start | bytes 196616 | tf_op jit(solution)/shard_map/ppermute | solution.py:12
  110.7 16.1 %collective-permute-start.9 = (f32[16,1024]{1,0:T(8,128)S(1)}, f32[16,1024]{1,0:T(8,128)S(1)}, u32[]{:S(2)}, u32[]{:S(2)}) collective-permute-start(f32[16,1024]{1,0:T(8,128)S(1)} %get-tuple-element.64), channel_id=1, source_target_pairs={{8,0},{16,8},{24,16},{32,24},{40,32},{48,40},{56,48},{64,56},{72,6... | collective-permute-start | bytes 196616 | tf_op jit(solution)/shard_map/ppermute | solution.py:12
  113.5 15.2 %collective-permute-start.8 = (f32[16,1024]{1,0:T(8,128)S(1)}, f32[16,1024]{1,0:T(8,128)S(1)}, u32[]{:S(2)}, u32[]{:S(2)}) collective-permute-start(f32[16,1024]{1,0:T(8,128)S(1)} %multiply_add_fusion.12), channel_id=1, source_target_pairs={{0,512},{8,520},{16,528},{24,536},{32,544},{40,552},{48,560},{56,5... | collective-permute-start | bytes 196616 | tf_op jit(solution)/shard_map/ppermute | solution.py:12
  128.8 10.4 %collective-permute-start.11 = (f32[16,1024]{1,0:T(8,128)S(1)}, f32[16,1024]{1,0:T(8,128)S(1)}, u32[]{:S(2)}, u32[]{:S(2)}) collective-permute-start(f32[16,1024]{1,0:T(8,128)S(1)} %get-tuple-element.135), channel_id=1, source_target_pairs={{16,0},{24,8},{32,16},{40,24},{48,32},{56,40},{64,48},{72,56},{80,... | collective-permute-start | bytes 196616 | tf_op jit(solution)/shard_map/ppermute | solution.py:12
  139.2 7.4 %collective-permute-start.12 = (f32[16,1024]{1,0:T(8,128)S(1)}, f32[16,1024]{1,0:T(8,128)S(1)}, u32[]{:S(2)}, u32[]{:S(2)}) collective-permute-start(f32[16,1024]{1,0:T(8,128)S(1)} %multiply_add_fusion.9), channel_id=1, source_target_pairs={{32,0},{40,8},{48,16},{56,24},{64,32},{72,40},{80,48},{88,56},{96,... | collective-permute-start | bytes 196616 | tf_op jit(solution)/shard_map/ppermute | solution.py:12
  146.6 10.8 %collective-permute-start.13 = (f32[16,1024]{1,0:T(8,128)S(1)}, f32[16,1024]{1,0:T(8,128)S(1)}, u32[]{:S(2)}, u32[]{:S(2)}) collective-permute-start(f32[16,1024]{1,0:T(8,128)S(1)} %multiply_add_fusion.8), channel_id=1, source_target_pairs={{64,0},{72,8},{80,16},{88,24},{96,32},{104,40},{112,48},{120,56},{... | collective-permute-start | bytes 196616 | tf_op jit(solution)/shard_map/ppermute | solution.py:12
  157.4 64.7 %copy-start.2 = (f32[16,16,1024]{2,1,0:T(8,128)S(1)}, f32[16,16,1024]{2,1,0:T(8,128)}, u32[]{:S(2)}) copy-start(f32[16,16,1024]{2,1,0:T(8,128)} %get-tuple-element.127) | copy-start | bytes 3145732
  157.4 10.2 %collective-permute-start.14 = (f32[16,1024]{1,0:T(8,128)S(1)}, f32[16,1024]{1,0:T(8,128)S(1)}, u32[]{:S(2)}, u32[]{:S(2)}) collective-permute-start(f32[16,1024]{1,0:T(8,128)S(1)} %multiply_add_fusion.7), channel_id=1, source_target_pairs={{128,0},{136,8},{144,16},{152,24},{160,32},{168,40},{176,48},{184,... | collective-permute-start | bytes 196616 | tf_op jit(solution)/shard_map/ppermute | solution.py:12
  167.6 28.0 %collective-permute-start.15 = (f32[16,1024]{1,0:T(8,128)S(1)}, f32[16,1024]{1,0:T(8,128)S(1)}, u32[]{:S(2)}, u32[]{:S(2)}) collective-permute-start(f32[16,1024]{1,0:T(8,128)S(1)} %multiply_add_fusion.6), channel_id=1, source_target_pairs={{256,0},{264,8},{272,16},{280,24},{288,32},{296,40},{304,48},{312,... | collective-permute-start | bytes 196616 | tf_op jit(solution)/shard_map/ppermute | solution.py:12
  195.6 25.3 %collective-permute-start.16 = (f32[16,1024]{1,0:T(8,128)S(1)}, f32[16,1024]{1,0:T(8,128)S(1)}, u32[]{:S(2)}, u32[]{:S(2)}) collective-permute-start(f32[16,1024]{1,0:T(8,128)S(1)} %multiply_add_fusion.5), channel_id=1, source_target_pairs={{512,0},{520,8},{528,16},{536,24},{544,32},{552,40},{560,48},{568,... | collective-permute-start | bytes 196616 | tf_op jit(solution)/shard_map/ppermute | solution.py:12
  224.0 5.7 %copy-start.1 = (f32[16,16,1024]{2,1,0:T(8,128)S(1)}, f32[16,16,1024]{2,1,0:T(8,128)}, u32[]{:S(2)}) copy-start(f32[16,16,1024]{2,1,0:T(8,128)} %get-tuple-element.129) | copy-start | bytes 3145732
  229.7 3.2 %copy-start.9 = (f32[1024]{0:T(1024)S(1)}, f32[1024]{0:T(1024)}, u32[]{:S(2)}) copy-start(f32[1024]{0:T(1024)} %param.15) | copy-start | bytes 12292
  234.2 5.7 %collective-permute-start.17 = (f32[3,2,1024]{2,1,0:T(2,128)S(1)}, f32[3,2,1024]{2,1,0:T(2,128)S(1)}, u32[]{:S(2)}, u32[]{:S(2)}) collective-permute-start(f32[3,2,1024]{2,1,0:T(2,128)S(1)} %slice.58), channel_id=1, source_target_pairs={{8,0},{16,8},{24,16},{32,24},{40,32},{48,40},{56,48},{64,56},{72,6... | collective-permute-start | bytes 73736 | tf_op jit(solution)/shard_map/ppermute | solution.py:12
  (5 other events, 10.1 us)
